TPU v7x, 32 devices: a whole 2x2x4 slice. The times are simulated.
32 devices in a mesh: group: 2 (over x), strip: 16 (over z, y, core).
Axes of the slice: x: 2, y: 2, z: 4, core: 2. Of those that a mesh axis runs over, the one named last changes fastest.
Arguments:
- strip_fields: float32 [3, 64, 128, 128], P(None, ('group', 'strip')), may hold values from -18 to 18
- strip_riser: int32 [64, 1], P('group'), may hold values from 0 to 3; in each aligned block of 2 rows (0 to 1, 2 to 3, ...) at most 2 rows name the same one
- strip_node: int32 [64], P('group'), may hold values from 0 to 1023
- riser_owner: int32 [2, 4], P('group'), may hold values from 0 to 15, as said below
- pivot_inv: float32 [32, 8, 128, 128], P(('group', 'strip')), may hold values from -0.2 to 1
- lower_block: float32 [32, 7, 128, 128], P(('group', 'strip')), may hold values from -0.109375 to 0.109375
- upper_block: float32 [32, 7, 128, 128], P(('group', 'strip')), may hold values from -0.109375 to 0.109375
Outputs:
- vorticity: float32 [64, 128, 128], P(('group', 'strip'))
- displacement: float32 [32, 16, 1024], P(('group', 'strip'))
Inputs may be any that keep to these rules, and one draw needn't show every extreme that they name: `strip_riser`: in each aligned block of 2 strips (the strips of one device) no riser is named more than 2 times, and some block names one riser exactly 2 times. `riser_owner`: the 4 owners in a row are distinct devices.
All inputs are finite; a program needn't handle non-finite values.
Results may differ from a plain program's by a relative error of at most 0.0003.
Values sent between devices are 32-bit elements; how exact they have to be, the bound alone decides.
No kernel may reach another device: no remote copies, remote signals or barrier semaphores. Data moves between devices by JAX's collectives and lax.ppermute only.
A program may use at most 64 MiB of HBM per device.

v0:
```python
import jax
import jax.numpy as jnp
from jax import lax
from jax.sharding import PartitionSpec as P

NSUB = 8
COUPLED = 2
TIME_STEP = 0.25
VISCOSITY = 0.05
COUPLING = 0.5
EXACT_DOT = lax.Precision.HIGHEST


def make_kernels(grid_cells):
    centre = jnp.arange(grid_cells, dtype=jnp.float32) - grid_cells / 2.0 + 0.5
    near_x = (centre / (grid_cells / 16.0))[None, :]
    near_y = (centre / (grid_cells / 16.0))[:, None]
    bell_near = jnp.exp(-(near_x * near_x + near_y * near_y) / 2.0)
    source_x = -near_x * bell_near
    source_y = -near_y * bell_near
    wide_x = (centre / (grid_cells / 8.0))[None, :]
    wide_y = (centre / (grid_cells / 8.0))[:, None]
    bell_wide = jnp.exp(-(wide_x * wide_x + wide_y * wide_y) / 2.0)
    lift_kernel = -wide_x * bell_wide
    drag_kernel = wide_y * bell_wide
    lift_kernel = lift_kernel / jnp.sqrt(jnp.sum(lift_kernel * lift_kernel))
    drag_kernel = drag_kernel / jnp.sqrt(jnp.sum(drag_kernel * drag_kernel))
    return (source_x, source_y, lift_kernel, drag_kernel)


def strip_step(vorticity, flow_x, flow_y, motion, kernels, substeps):
    source_x, source_y, lift_kernel, drag_kernel = kernels
    halves = motion.reshape(motion.shape[0], 2, substeps)
    earlier = jnp.concatenate([jnp.zeros_like(halves[:, :, :1]), halves[:, :, :-1]], axis=2)
    velocity = halves - earlier
    lift_rows = []
    drag_rows = []
    for substep in range(substeps):
        right_cell = jnp.roll(vorticity, -1, axis=2)
        left_cell = jnp.roll(vorticity, 1, axis=2)
        upper_cell = jnp.roll(vorticity, -1, axis=1)
        lower_cell = jnp.roll(vorticity, 1, axis=1)
        laplacian = right_cell + left_cell + upper_cell + lower_cell - 4.0 * vorticity
        tendency = (
            VISCOSITY * laplacian
            - flow_x * (0.5 * (right_cell - left_cell))
            - flow_y * (0.5 * (upper_cell - lower_cell))
        )
        forcing = (
            velocity[:, 0, substep][:, None, None] * source_x
            - velocity[:, 1, substep][:, None, None] * source_y
        )
        vorticity = vorticity + TIME_STEP * tendency + COUPLING * forcing
        lift_rows.append(jnp.sum(vorticity * lift_kernel, axis=(1, 2)))
        drag_rows.append(jnp.sum(vorticity * drag_kernel, axis=(1, 2)))
    return (vorticity, jnp.stack(lift_rows + drag_rows, axis=1))


def apply_block(vectors, matrix):
    return lax.dot_general(vectors, matrix, (((1,), (1,)), ((), ())), precision=EXACT_DOT)


def first_contract(left_side, right_side):
    return lax.dot_general(left_side, right_side, (((0,), (0,)), ((), ())), precision=EXACT_DOT)


def beam_solve(beam_load, pivot_inv, lower_block, upper_block):
    block_count = pivot_inv.shape[0]
    block_size = pivot_inv.shape[1]
    blocks = beam_load.reshape(beam_load.shape[0], block_count, block_size)
    carried = [blocks[:, 0]]
    for block_index in range(1, block_count):
        pivoted = apply_block(carried[-1], pivot_inv[block_index - 1])
        carried.append(blocks[:, block_index] - apply_block(pivoted, lower_block[block_index - 1]))
    solved = [apply_block(carried[-1], pivot_inv[block_count - 1])]
    for block_index in range(block_count - 2, -1, -1):
        remainder = carried[block_index] - apply_block(solved[0], upper_block[block_index])
        solved.insert(0, apply_block(remainder, pivot_inv[block_index]))
    return jnp.concatenate(solved, axis=1)


def local(strip_fields, strip_riser, strip_node, riser_owner, pivot_inv, lower_block, upper_block):
    devices = lax.axis_size("strip")
    position = lax.axis_index("strip")
    per_device = strip_fields.shape[1]
    grid_cells = strip_fields.shape[2]
    node_count = pivot_inv.shape[1] * pivot_inv.shape[2]
    riser_count = riser_owner.shape[1]
    substeps = NSUB
    total_strips = per_device * devices * lax.axis_size("group")
    kernels = make_kernels(grid_cells)
    riser_match = (
        strip_riser[:, 0][:, None] == jnp.arange(riser_count, dtype=jnp.int32)[None, :]
    ).astype(jnp.int32)
    owner_index = jnp.sum(riser_match * riser_owner[0][None, :], axis=1)
    owned_here = owner_index == position
    node_hit = (
        owned_here[:, None]
        & (strip_node[:, None] == jnp.arange(node_count, dtype=jnp.int32)[None, :])
    ).astype(jnp.float32)
    local_owner = lax.dynamic_slice_in_dim(owner_index, position * per_device, per_device)
    local_node = lax.dynamic_slice_in_dim(strip_node, position * per_device, per_device)
    top_taper = 1.0 - jnp.arange(node_count, dtype=jnp.float32) / node_count
    vorticity = strip_fields[0]
    flow_x = strip_fields[1]
    flow_y = strip_fields[2]
    motion = jnp.zeros((per_device, 2 * substeps), jnp.float32)
    displacement = jnp.zeros((2 * substeps, node_count), jnp.float32)
    for coupled_step in range(COUPLED):
        vorticity, force_rows = strip_step(vorticity, flow_x, flow_y, motion, kernels, substeps)
        partial_drag = jnp.sum(force_rows[:, substeps:], axis=0)
        total_drag = lax.psum(partial_drag, ("group", "strip"))
        offset = total_drag / jnp.sqrt(jnp.float32(total_strips))
        beam_load = first_contract(
            lax.all_gather(force_rows, "strip", axis=0, tiled=True), node_hit
        )
        displacement = beam_solve(beam_load, pivot_inv[0], lower_block[0], upper_block[0])
        displacement = displacement.at[substeps:, :].add(offset[:, None] * top_taper[None, :])
        if coupled_step + 1 < COUPLED:
            every_owner = lax.all_gather(displacement[None], "strip", axis=0, tiled=True)
            chosen = jnp.take(every_owner, local_owner, axis=0)
            node_pick = jnp.broadcast_to(local_node[:, None, None], (per_device, 2 * substeps, 1))
            motion = jnp.take_along_axis(chosen, node_pick, axis=2)[:, :, 0]
    return (vorticity, displacement[None])


def solution(mesh):
    in_specs = (
        P(None, ("group", "strip"), None, None),
        P("group", None),
        P("group"),
        P("group", None),
        P(("group", "strip"), None, None, None),
        P(("group", "strip"), None, None, None),
        P(("group", "strip"), None, None, None),
    )
    out_specs = (P(("group", "strip"), None, None), P(("group", "strip"), None, None))
    return jax.shard_map(local, mesh=mesh, in_specs=in_specs, out_specs=out_specs, check_vma=False)
```

profile of v0, /device:TPU:0, one launch (start us, length us, event | category | flops | bytes accessed | tf_op | source)
XLA Modules:
  0.0 231.5 jit_solution(9136430588047142506)
XLA Ops:
  15.9 42.0 %psum.14 = f32[8]{0:T(128)S(1)} all-reduce(f32[8]{0:T(128)S(1)} %reduce_sum.352), channel_id=1, replica_groups=mesh['group'=2,'strip'=16] {'group','strip'}, use_global_device_ids=true, to_apply=%region_20.21 | all-reduce | flops 8 | bytes 64 | tf_op jit(solution)/shard_map/psum | solution.py:112
  58.8 21.0 %all-gather = f32[16,2,16]{2,1,0:T(2,128)S(1)} all-gather(f32[1,2,16]{2,1,0:T(2,128)S(1)} %bitcast.564), channel_id=1, replica_groups=mesh['group'=2,'strip'=16] {'strip'}, dimensions={0}, use_global_device_ids=true | all-gather | bytes 2176 | tf_op jit(solution)/shard_map/all_gather | solution.py:115
  82.5 1.1 convolution_subtract_fusion.27
  83.6 1.1 fusion.159
  84.7 1.1 convolution_subtract_fusion.26
  85.8 1.1 fusion.149
  86.9 1.1 convolution_subtract_fusion.25
  88.0 1.1 fusion.139
  89.0 1.1 convolution_subtract_fusion.24
  90.1 1.1 fusion.129
  91.2 1.1 convolution_subtract_fusion.23
  92.2 1.1 fusion.119
  93.3 1.1 convolution_subtract_fusion.22
  94.3 1.1 fusion.109
  95.4 1.1 convolution_subtract_fusion.21
  96.5 1.1 fusion.99
  102.2 33.8 %all-gather.4.cloned.1.call-done = f32[16,16,1024]{2,1,0:T(8,128)} async-done(((f32[1,16,1024]{2,1,0:T(8,128)}), f32[16,16,1024]{2,1,0:T(8,128)}) %all-gather.4.cloned.1.call-update) | async-done | bytes 1048592 | tf_op jit(solution)/shard_map/all_gather | solution.py:120
  136.0 1.8 gather_fusion
  142.2 1.1 multiply_reduce_fusion.7
  144.2 38.9 %psum.15 = f32[8]{0:T(128)S(1)} all-reduce(f32[8]{0:T(128)S(1)} %reduce_sum.369), channel_id=1, replica_groups=mesh['group'=2,'strip'=16] {'group','strip'}, use_global_device_ids=true, to_apply=%region_38.39 | all-reduce | flops 8 | bytes 64 | tf_op jit(solution)/shard_map/psum | solution.py:112
  183.9 20.6 %all-gather.1 = f32[16,2,16]{2,1,0:T(2,128)S(1)} all-gather(f32[1,2,16]{2,1,0:T(2,128)S(1)} %bitcast.565), channel_id=1, replica_groups=mesh['group'=2,'strip'=16] {'strip'}, dimensions={0}, use_global_device_ids=true | all-gather | bytes 2176 | tf_op jit(solution)/shard_map/all_gather | solution.py:115
  205.8 1.1 convolution_subtract_fusion.13
  206.9 1.1 fusion.155
  208.0 1.1 convolution_subtract_fusion.12
  210.1 1.1 convolution_subtract_fusion.11
  211.2 1.1 fusion.135
  212.2 1.1 convolution_subtract_fusion.10
  213.3 1.1 fusion.125
  214.3 1.1 convolution_subtract_fusion.9
  216.5 1.1 convolution_subtract_fusion.8
  218.6 1.1 convolution_subtract_fusion.7
  219.6 1.1 fusion.97
  (220 shorter events, 29.4 us)
Async XLA Ops:
  7.2 128.8 %all-gather.4.cloned.1.call-start = ((), (), s32[]{:S(2)}) async-start(), calls=%async_computation | async-start | bytes 1114112 | tf_op jit(solution)/shard_map/all_gather | solution.py:120
  8.3 1.0 copy-start
  79.8 0.7 copy-start.6
  79.8 0.7 copy-start.7
  80.5 0.7 copy-start.5
  84.7 12.9 %copy-start.2 = (f32[1,7,128,128]{3,2,1,0:T(8,128)S(1)}, f32[1,7,128,128]{3,2,1,0:T(8,128)}, u32[]{:S(2)}) copy-start(f32[1,7,128,128]{3,2,1,0:T(8,128)} %param.17) | copy-start | bytes 1376260
  85.8 12.0 %copy-start.1 = (f32[1,8,128,128]{3,2,1,0:T(8,128)S(1)}, f32[1,8,128,128]{3,2,1,0:T(8,128)}, u32[]{:S(2)}) copy-start(f32[1,8,128,128]{3,2,1,0:T(8,128)} %param.15) | copy-start | bytes 1572868
  100.9 0.6 copy-start.3
  224.1 0.6 copy-start.4
Sparse Core Ops, SparseCore 0:
  101.7 34.2 all-gather.3
where the time goes:
time: 233 us; the launch traced here: 232 us
  blocking collectives  123 us (53%)
  matrix products  38.5 us (17%)
  waiting for transfers between devices  33.8 us (15%)
  between operations  16.3 us (7%)
  local copies, waits for them, and re-layouts  14.4 us (6%)
  other arithmetic  5.94 us (3%)
    psum x2, blocking collectives, local(): total_drag = lax.psum(partial_drag, ('group', 'strip'))  80.9 us
    all_gather x2, blocking collectives, local(): lax.all_gather(force_rows, 'strip', axis=0, tiled=True)  41.6 us
    dot_general x58, matrix products, apply_block(): lax.dot_general(vectors, matrix, (((1,), (1,)), ((), ())), precision=EXAC...  38 us
    all_gather x1, waiting for transfers between devices, local(): lax.all_gather(displacement[None], 'strip', axis=0, tiled=True)  33.8 us
  transfers between devices with their start and end apart: 1, of which 1 were waited for; matrix products, arithmetic and copies ran while one was open for 0% of the time, Pallas kernels for 0%

commit v1 on v0

--- a/solution.py
+++ b/solution.py
@@ -109,7 +109,7 @@
     for coupled_step in range(COUPLED):
         vorticity, force_rows = strip_step(vorticity, flow_x, flow_y, motion, kernels, substeps)
         partial_drag = jnp.sum(force_rows[:, substeps:], axis=0)
-        total_drag = lax.psum(partial_drag, ("group", "strip"))
+        total_drag = jnp.sum(lax.all_gather(partial_drag, ("group", "strip")), axis=0)
         offset = total_drag / jnp.sqrt(jnp.float32(total_strips))
         beam_load = first_contract(
             lax.all_gather(force_rows, "strip", axis=0, tiled=True), node_hit

time: 233 us -> 234 us (level)
    psum x2 -> x0, blocking collectives: 80.9 us -> none  [local(): total_drag = lax.psum(partial_drag, ('group', 'strip'))]
    unnamed x0 -> x2, blocking collectives: none -> 80.8 us
where the time goes in v1:
time: 234 us; the launch traced here: 232 us
  blocking collectives  122 us (52%)
  matrix products  38.5 us (16%)
  waiting for transfers between devices  33.8 us (14%)
  between operations  16.3 us (7%)
  local copies, waits for them, and re-layouts  15 us (6%)
  other arithmetic  6 us (3%)
    unnamed x2, blocking collectives  80.8 us
    all_gather x2, blocking collectives, local(): lax.all_gather(force_rows, 'strip', axis=0, tiled=True)  41.6 us
    dot_general x58, matrix products, apply_block(): lax.dot_general(vectors, matrix, (((1,), (1,)), ((), ())), precision=EXAC...  38 us
    all_gather x1, waiting for transfers between devices, local(): lax.all_gather(displacement[None], 'strip', axis=0, tiled=True)  33.8 us
  transfers between devices with their start and end apart: 1, of which 1 were waited for; matrix products, arithmetic and copies ran while one was open for 0% of the time, Pallas kernels for 0%

profile of v1, /device:TPU:0, one launch (start us, length us, event | category | flops | bytes accessed | tf_op | source)
XLA Modules:
  0.0 232.2 jit_solution(10416403958677210791)
XLA Ops:
  16.2 42.0 %all-reduce.1 = f32[256]{0:T(256)S(1)} all-reduce(f32[256]{0:T(256)S(1)} %dynamic-update-slice.8), channel_id=2, replica_groups=mesh['group'=2,'strip'=16] {'group','strip'}, use_global_device_ids=true, to_apply=%add.1 | all-reduce | flops 256 | bytes 2048
  59.1 21.0 %all-gather.2 = f32[16,2,16]{2,1,0:T(2,128)S(1)} all-gather(f32[1,2,16]{2,1,0:T(2,128)S(1)} %bitcast.564), channel_id=1, replica_groups=mesh['group'=2,'strip'=16] {'strip'}, dimensions={0}, use_global_device_ids=true | all-gather | bytes 2176 | tf_op jit(solution)/shard_map/all_gather | solution.py:115
  82.9 1.1 convolution_subtract_fusion.27
  83.9 1.1 fusion.159
  85.0 1.1 convolution_subtract_fusion.26
  86.2 1.1 fusion.149
  87.3 1.1 convolution_subtract_fusion.25
  88.3 1.1 fusion.139
  89.4 1.1 convolution_subtract_fusion.24
  90.4 1.1 fusion.129
  91.5 1.1 convolution_subtract_fusion.23
  92.6 1.1 fusion.119
  93.6 1.1 convolution_subtract_fusion.22
  94.7 1.1 fusion.109
  95.7 1.1 convolution_subtract_fusion.21
  96.8 1.1 fusion.99
  102.5 33.8 %all-gather.6.cloned.1.call-done = f32[16,16,1024]{2,1,0:T(8,128)} async-done(((f32[1,16,1024]{2,1,0:T(8,128)}), f32[16,16,1024]{2,1,0:T(8,128)}) %all-gather.6.cloned.1.call-update) | async-done | bytes 1048592 | tf_op jit(solution)/shard_map/all_gather | solution.py:120
  136.3 1.8 gather_fusion
  142.5 1.1 multiply_reduce_fusion.7
  144.7 38.9 %all-reduce.2 = f32[256]{0:T(256)S(1)} all-reduce(f32[256]{0:T(256)S(1)} %dynamic-update-slice.9), channel_id=3, replica_groups=mesh['group'=2,'strip'=16] {'group','strip'}, use_global_device_ids=true, to_apply=%add.2 | all-reduce | flops 256 | bytes 2048
  184.6 20.6 %all-gather.3 = f32[16,2,16]{2,1,0:T(2,128)S(1)} all-gather(f32[1,2,16]{2,1,0:T(2,128)S(1)} %bitcast.565), channel_id=1, replica_groups=mesh['group'=2,'strip'=16] {'strip'}, dimensions={0}, use_global_device_ids=true | all-gather | bytes 2176 | tf_op jit(solution)/shard_map/all_gather | solution.py:115
  206.5 1.1 convolution_subtract_fusion.13
  207.6 1.1 fusion.155
  208.6 1.1 convolution_subtract_fusion.12
  210.8 1.1 convolution_subtract_fusion.11
  211.8 1.1 fusion.135
  212.9 1.1 convolution_subtract_fusion.10
  213.9 1.1 fusion.125
  215.0 1.1 convolution_subtract_fusion.9
  217.1 1.1 convolution_subtract_fusion.8
  219.3 1.1 convolution_subtract_fusion.7
  220.3 1.1 fusion.97
  (228 shorter events, 30.1 us)
Async XLA Ops:
  7.2 129.1 %all-gather.6.cloned.1.call-start = ((), (), s32[]{:S(2)}) async-start(), calls=%async_computation | async-start | bytes 1114112 | tf_op jit(solution)/shard_map/all_gather | solution.py:120
  8.3 1.0 copy-start
  80.1 0.7 copy-start.6
  80.1 0.7 copy-start.7
  80.9 0.7 copy-start.5
  85.0 12.9 %copy-start.2 = (f32[1,7,128,128]{3,2,1,0:T(8,128)S(1)}, f32[1,7,128,128]{3,2,1,0:T(8,128)}, u32[]{:S(2)}) copy-start(f32[1,7,128,128]{3,2,1,0:T(8,128)} %param.17) | copy-start | bytes 1376260
  86.1 12.0 %copy-start.1 = (f32[1,8,128,128]{3,2,1,0:T(8,128)S(1)}, f32[1,8,128,128]{3,2,1,0:T(8,128)}, u32[]{:S(2)}) copy-start(f32[1,8,128,128]{3,2,1,0:T(8,128)} %param.15) | copy-start | bytes 1572868
  101.2 0.6 copy-start.3
  224.7 0.6 copy-start.4
Sparse Core Ops, SparseCore 0:
  102.0 34.2 all-gather.5
